TPU v7x, 128 devices: a whole 4x4x4 slice. The times are simulated.
128 devices in a mesh: dp: 32 (over y, x, core), mp: 4 (over z).
Axes of the slice: x: 4, y: 4, z: 4, core: 2. Of those that a mesh axis runs over, the one named last changes fastest.
Arguments:
- hidden: bfloat16 [4096, 2560], P('dp', 'mp'), may hold values from -6 to 6
- norm_gain: bfloat16 [2560], replicated, may hold values from 0.5 to 1.5
- shared_gate: bfloat16 [2560, 3072], P(None, 'mp'), may hold values from -0.125 to 0.125
- shared_up: bfloat16 [2560, 3072], P(None, 'mp'), may hold values from -0.125 to 0.125
- shared_down: bfloat16 [3072, 2560], P('mp'), may hold values from -0.109375 to 0.109375
- expert_gate: bfloat16 [64, 2560, 1536], P('dp', None, 'mp'), may hold values from -0.125 to 0.125
- expert_up: bfloat16 [64, 2560, 1536], P('dp', None, 'mp'), may hold values from -0.125 to 0.125
- expert_down: bfloat16 [64, 1536, 2560], P('dp', 'mp'), may hold values from -0.15625 to 0.15625
- adapter_in: bfloat16 [64, 3072, 16], P('dp', 'mp'), may hold values from -0.109375 to 0.109375
- adapter_out: bfloat16 [64, 16, 2560], P('dp'), may hold values from -1.5 to 1.5
- active: int32 [16], replicated, may hold values from 0 to 63, as said below
- lengths: int32 [64], replicated, may hold values from 1 to 1024, 4096 in all
- request_adapter: int32 [64], replicated, may hold values from 0 to 15
- routes: int32 [4096, 6], P('dp'), may hold values from 0 to 63, all different within a row; in each aligned block of 128 rows (0 to 127, 128 to 255, ...) at most 16 rows name the same one
- route_weights: float32 [4096, 6], P('dp'), may hold values from 0.05 to 0.35
Outputs:
- layer_out: bfloat16 [4096, 2560], P('dp', 'mp')
Inputs may be any that keep to these rules, and one draw needn't show every extreme that they name: `active`: the entries are distinct. `routes`: within the 128 rows of one index of dp no expert is named more than 16 times, and that many is reached; a row names distinct experts.
All inputs are finite; a program needn't handle non-finite values.
Results may differ from a plain program's by a relative error of at most 0.015.
Values may be sent and summed in bfloat16 or wider, within the bound.
No kernel may reach another device: no remote copies, remote signals or barrier semaphores. Data moves between devices by JAX's collectives and lax.ppermute only.
A program may use at most 128 MiB of HBM per device.

v0:
```python
import jax
import jax.numpy as jnp
from jax import lax
from jax.sharding import PartitionSpec as P


def experts_apply(slots_in, expert_gate, expert_up, expert_down):
    gate_val = jnp.einsum(
        "sjcd,jdf->sjcf", slots_in, expert_gate, preferred_element_type=jnp.float32
    )
    up_val = jnp.einsum("sjcd,jdf->sjcf", slots_in, expert_up, preferred_element_type=jnp.float32)
    inner = (jax.nn.silu(gate_val) * up_val).astype(jnp.bfloat16)
    return jnp.einsum("sjcf,jfd->sjcd", inner, expert_down, preferred_element_type=jnp.float32)


def body(
    hidden,
    norm_gain,
    shared_gate,
    shared_up,
    shared_down,
    expert_gate,
    expert_up,
    expert_down,
    adapter_in,
    adapter_out,
    active,
    lengths,
    request_adapter,
    routes,
    route_weights,
):
    tok_rows = routes.shape[0]
    top_count = routes.shape[1]
    dp_count = lax.axis_size("dp")
    mp_count = lax.axis_size("mp")
    dp_index = lax.axis_index("dp")
    mp_index = lax.axis_index("mp")
    local_experts = expert_gate.shape[0]
    total_experts = local_experts * dp_count
    capacity = mp_count * max(1, tok_rows * top_count * 4 // (total_experts * mp_count * 3))
    col_width = hidden.shape[1]
    col_start = mp_index * col_width
    active_count = active.shape[0]
    rank_width = adapter_in.shape[2]
    local_adapters = adapter_in.shape[0]
    owned_ids = dp_index * local_adapters + jnp.arange(local_adapters, dtype=jnp.int32)
    selector = (active[:, None] == owned_ids[None, :]).astype(jnp.bfloat16)
    out_cols = lax.dynamic_slice_in_dim(adapter_out, col_start, col_width, axis=2)
    picked_in = jnp.einsum(
        "ji,isr->jsr", selector, adapter_in, preferred_element_type=jnp.float32
    ).astype(jnp.bfloat16)
    picked_out = jnp.einsum(
        "ji,ird->jrd", selector, out_cols, preferred_element_type=jnp.float32
    ).astype(jnp.bfloat16)
    picked_in, picked_out = lax.psum((picked_in, picked_out), "dp")
    gathered = lax.all_gather(hidden, "mp", axis=1, tiled=True)
    values = gathered.astype(jnp.float32)
    factor = lax.rsqrt(jnp.mean(values * values, axis=-1, keepdims=True) + 1e-06)
    normed = (values * factor * norm_gain.astype(jnp.float32)).astype(jnp.bfloat16)
    width = normed.shape[1]
    shared_lin = jnp.dot(normed, shared_gate, preferred_element_type=jnp.float32)
    shared_pre = jnp.dot(normed, shared_up, preferred_element_type=jnp.float32)
    shared_act = (jax.nn.silu(shared_lin) * shared_pre).astype(jnp.bfloat16)
    request_end = jnp.cumsum(lengths)
    positions = dp_index * tok_rows + jnp.arange(tok_rows, dtype=jnp.int32)
    request_of = jnp.sum((request_end[None, :] <= positions[:, None]).astype(jnp.int32), axis=1)
    request_hot = (
        request_of[:, None] == jnp.arange(lengths.shape[0], dtype=jnp.int32)[None, :]
    ).astype(jnp.int32)
    slot_of = jnp.sum(request_hot * request_adapter[None, :], axis=1)
    chosen = (slot_of[:, None] == jnp.arange(active_count, dtype=jnp.int32)[None, :]).astype(
        jnp.float32
    )
    in_matrix = jnp.transpose(picked_in, (1, 0, 2)).reshape(
        shared_act.shape[1], active_count * rank_width
    )
    lowrank = jnp.dot(shared_act, in_matrix, preferred_element_type=jnp.float32)
    lowrank_sel = jnp.sum(
        lowrank.reshape(tok_rows, active_count, rank_width) * chosen[:, :, None], axis=1
    )
    lowrank_sel = lax.psum(lowrank_sel, "mp")
    lowrank = (chosen[:, :, None] * lowrank_sel[:, None, :]).reshape(
        tok_rows, active_count * rank_width
    )
    adapted = jnp.dot(
        lowrank,
        picked_out.reshape(active_count * rank_width, col_width).astype(jnp.float32),
        precision=lax.Precision.HIGHEST,
    )
    flat_routes = routes.reshape(-1)
    expert_hot = (
        flat_routes[:, None] == jnp.arange(total_experts, dtype=jnp.int32)[None, :]
    ).astype(jnp.int32)
    earlier = jnp.cumsum(expert_hot, axis=0) - expert_hot
    position = jnp.sum(earlier * expert_hot, axis=1)
    slot_index = (flat_routes * capacity + position).reshape(tok_rows, top_count)
    slot_count = total_experts * capacity
    slot_hit = slot_index[:, :, None] == jnp.arange(slot_count, dtype=jnp.int32)[None, None, :]
    dispatch = jnp.any(slot_hit, axis=1).astype(jnp.bfloat16)
    send_rows = jnp.einsum(
        "ts,td->sd", dispatch, normed, preferred_element_type=jnp.float32
    ).astype(jnp.bfloat16)
    send_rows = send_rows.reshape(dp_count, local_experts, capacity, width)
    returned = lax.all_to_all(
        experts_apply(
            lax.all_to_all(send_rows, "dp", split_axis=0, concat_axis=0, tiled=True),
            expert_gate,
            expert_up,
            expert_down,
        ).astype(jnp.bfloat16),
        "dp",
        split_axis=0,
        concat_axis=0,
        tiled=True,
    )
    returned = returned.reshape(slot_count, width)
    combine = jnp.sum(jnp.where(slot_hit, route_weights[:, :, None], 0.0), axis=1)
    combine_hi = combine.astype(jnp.bfloat16)
    combine_lo = (combine - combine_hi.astype(jnp.float32)).astype(jnp.bfloat16)
    routed = jnp.dot(combine_hi, returned, preferred_element_type=jnp.float32) + jnp.dot(
        combine_lo, returned, preferred_element_type=jnp.float32
    )
    partial_out = jnp.dot(shared_act, shared_down, preferred_element_type=jnp.float32) + routed
    own_cols = lax.dynamic_slice_in_dim(partial_out, col_start, col_width, axis=1) + adapted
    partial_out = lax.dynamic_update_slice_in_dim(partial_out, own_cols, col_start, axis=1)
    return lax.psum_scatter(partial_out.astype(jnp.bfloat16), "mp", scatter_dimension=1, tiled=True)


def solution(mesh):
    in_specs = (
        P("dp", "mp"),
        P(),
        P(None, "mp"),
        P(None, "mp"),
        P("mp", None),
        P("dp", None, "mp"),
        P("dp", None, "mp"),
        P("dp", "mp", None),
        P("dp", "mp", None),
        P("dp", None, None),
        P(),
        P(),
        P(),
        P("dp", None),
        P("dp", None),
    )
    out_specs = P("dp", "mp")
    return jax.shard_map(body, mesh=mesh, in_specs=in_specs, out_specs=out_specs, check_vma=False)
```

profile of v0, /device:TPU:0, one launch (start us, length us, event | category | flops | bytes accessed | tf_op | source)
XLA Modules:
  0.0 315.9 jit_solution(4285871344129331172)
XLA Ops:
  6.5 0.0 copy-start
  6.5 0.8 copy.60
  7.4 0.1 eq.85
  7.5 0.1 eq.81
  7.7 1.8 reduce-window.18
  9.5 0.3 slice_reduce_fusion
  9.8 0.1 fusion.34
  9.9 0.1 reduce_sum.58
  10.1 0.1 copy.63
  10.1 0.7 multiply_add_fusion
  10.8 0.5 fusion.9
  11.3 14.9 %all_gather.3 = bf16[128,2560]{1,0:T(8,128)(2,1)S(1)} all-gather(bf16[128,640]{1,0:T(8,128)(2,1)} %param.15), channel_id=1, replica_groups=mesh['dp'=32,'mp'=4] {'mp'}, dimensions={1}, use_global_device_ids=true | all-gather | bytes 819200 | tf_op jit(solution)/shard_map/all_gather | solution.py:57
  26.2 0.2 fusion.22
  26.5 0.7 convert_element_type.64
  27.2 1.6 convolution_convert_fusion.1
  28.8 0.0 copy-start.8
  28.8 69.5 %all_to_all.10 = bf16[32,2,16,2560]{3,2,1,0:T(8,128)(2,1)S(1)} all-to-all(bf16[32,2,16,2560]{3,2,1,0:T(8,128)(2,1)S(1)} %bitcast.98), channel_id=1, replica_groups=mesh['dp'=32,'mp'=4] {'dp'}, dimensions={0} | all-to-all | bytes 10485760 | tf_op jit(solution)/shard_map/all_to_all | solution.py:107
  98.3 0.0 copy-start.1
  98.3 2.3 copy-done.1
  100.6 0.0 copy-done.8
  100.6 2.9 fusion.3
  103.5 12.8 %fusion = bf16[32,2,16,2560]{3,2,0,1:T(8,128)(2,1)} fusion(bf16[2,384,2560]{2,1,0:T(8,128)(2,1)} %param.22, f32[2,32,16,384]{3,2,1,0:T(8,128)S(1)} %fusion.3, bf16[2,2560,384]{2,1,0:T(8,128)(2,1)} %param.21, bf16[32,2,16,2560]{3,2,1,0:T(8,128)(2,1)} %copy-done.1), kind=kOutput, calls=%fused_computation.2 | convolution fusion | flops 4031512576 | bytes 19922944 | tf_op jit(solution)/shard_map/sjcf,jfd->sjcd/dot_general | solution.py:13
  116.3 5.3 %copy.66 = bf16[32,2,16,2560]{3,2,1,0:T(8,128)(2,1)} copy(bf16[32,2,16,2560]{3,2,0,1:T(8,128)(2,1)} %fusion) | data formatting | bytes 10485760 | tf_op jit(solution)/shard_map/convert_element_type | solution.py:111
  121.5 0.0 copy-start.5
  121.5 5.0 %all-to-all-start.1 = ((bf16[32,2,16,2560]{3,2,1,0:T(8,128)(2,1)}), bf16[32,2,16,2560]{3,2,1,0:T(8,128)(2,1)}, u32[]{:S(2)}, u32[]{:S(2)}) async-start(bf16[32,2,16,2560]{3,2,1,0:T(8,128)(2,1)} %copy.66), calls=%async_computation.1 | async-start | bytes 10485760 | tf_op jit(solution)/shard_map/all_to_all | solution.py:105
  126.6 0.0 all-reduce.3.cloned.1.call-start
  126.6 0.0 copy-done.4
  126.6 0.0 copy-done.6
  126.6 0.4 fusion.25
  127.1 0.9 copy.95
  127.9 0.0 copy-done
  128.0 1.1 convolution_convert_fusion.3
  129.1 0.0 all-reduce.3.cloned.1.call-update
  129.1 0.2 reduce-scatter.4.cloned.1.call-start
  129.3 0.0 copy-done.7
  129.4 0.1 copy.67
  129.5 0.1 reduce-window.20
  129.5 0.1 reduce.1
  129.7 0.0 copy-start.9
  129.7 0.1 convert_reduce_fusion
  129.8 0.0 copy-done.10
  129.8 0.1 select_reduce_fusion.1
  129.9 0.0 copy-done.5
  129.9 0.4 select_reduce_fusion
  130.3 3.2 fusion.57
  133.5 0.0 copy-done.9
  133.5 0.0 copy-start.2
  133.5 0.8 fusion.26
  134.3 1.3 copy-done.2
  135.6 0.7 fusion.59
  136.3 131.0 %all-reduce.3.cloned.1.call-done = (bf16[16,16,640]{2,0,1:T(8,128)(2,1)}, bf16[16,16,768]{2,1,0:T(8,128)(2,1)}) async-done(((bf16[16,16,640]{2,0,1:T(8,128)(2,1)}, bf16[16,16,768]{2,1,0:T(8,128)(2,1)}), (bf16[16,16,640]{2,0,1:T(8,128)(2,1)}, bf16[16,16,768]{2,1,0:T(8,128)(2,1)})) %all-reduce.3.cloned.1.call-update) | async-done | bytes 720912 | tf_op jit(solution)/shard_map/psum | solution.py:56
  267.3 1.3 fusion.29
  268.6 10.8 %psum.22 = f32[128,16]{0,1:T(8,128)S(1)} all-reduce(f32[128,16]{0,1:T(8,128)S(1)} %fusion.29), channel_id=1, replica_groups=mesh['dp'=32,'mp'=4] {'mp'}, use_global_device_ids=true, to_apply=%region_11.12 | all-reduce | flops 2048 | bytes 16384 | tf_op jit(solution)/shard_map/psum | solution.py:82
  279.4 0.0 all-to-all-done.1
  279.4 3.3 %fusion.39 = f32[128,2560]{1,0:T(8,128)S(1)} fusion(bf16[1024,2560]{1,0:T(8,128)(2,1)} %bitcast.11, f32[128,1024]{1,0:T(8,128)S(1)} %select_reduce_fusion), kind=kOutput, calls=%fused_computation.53 | convolution fusion | flops 671219712 | bytes 7077888 | tf_op jit(solution)/shard_map/dot_general | solution.py:121
  282.7 0.0 copy-start.3
  282.7 3.5 %fusion.8 = f32[128,2560]{1,0:T(8,128)S(1)} fusion(f32[128,2560]{1,0:T(8,128)S(1)} %fusion.59, f32[128,2560]{1,0:T(8,128)S(1)} %fusion.39, bf16[1024,2560]{1,0:T(8,128)(2,1)} %bitcast.11, f32[128,1024]{1,0:T(8,128)S(1)} %select_reduce_fusion), kind=kOutput, calls=%fused_computation.11 | convolution fusion | flops 672268288 | bytes 9699328 | tf_op jit(solution)/shard_map/dot_general | solution.py:121
  286.2 0.0 copy-done.3
  286.2 0.4 fusion.28
  286.6 0.1 convert_element_type.80
  286.7 1.1 copy.75
  287.8 0.0 reduce-scatter.4.cloned.1.call-update
  287.8 19.6 %reduce-scatter.4.cloned.1.call-done = bf16[640,128]{1,0:T(8,128)(2,1)} async-done(((bf16[2560,128]{1,0:T(8,128)(2,1)}), bf16[640,128]{1,0:T(8,128)(2,1)}) %reduce-scatter.4.cloned.1.call-update) | async-done | bytes 163856
  307.4 1.7 copy.76
  (11 shorter events, 0.1 us)
Async XLA Ops:
  6.5 121.4 %copy-start = (bf16[2,16,2560]{2,1,0:T(8,128)(2,1)S(1)}, bf16[2,16,2560]{2,1,0:T(8,128)(2,1)}, u32[]{:S(2)}) copy-start(bf16[2,16,2560]{2,1,0:T(8,128)(2,1)} %param.24) | copy-start | bytes 491524
  28.8 71.8 %copy-start.8 = (bf16[2,2560,384]{2,1,0:T(8,128)(2,1)S(1)}, bf16[2,2560,384]{2,1,0:T(8,128)(2,1)}, u32[]{:S(2)}) copy-start(bf16[2,2560,384]{2,1,0:T(8,128)(2,1)} %param.20) | copy-start | bytes 11796484
  98.3 2.3 copy-start.1
  121.5 5.1 %copy-start.4 = (bf16[2,768,16]{1,2,0:T(8,128)(2,1)S(1)}, bf16[2,768,16]{1,2,0:T(8,128)(2,1)}, u32[]{:S(2)}) copy-start(bf16[2,768,16]{1,2,0:T(8,128)(2,1)} %param.23) | copy-start | bytes 147460
  121.5 5.1 %copy-start.6 = (s32[16]{0:T(128)S(1)}, s32[16]{0:T(128)}, u32[]{:S(2)}) copy-start(s32[16]{0:T(128)} %param.25) | copy-start | bytes 196
  121.5 7.8 %copy-start.7 = (s32[64]{0:T(128)S(1)}, s32[64]{0:T(128)}, u32[]{:S(2)}) copy-start(s32[64]{0:T(128)} %param.26) | copy-start | bytes 772
  121.5 8.2 %copy-start.10 = (s32[64]{0:T(128)S(1)}, s32[64]{0:T(128)}, u32[]{:S(2)}) copy-start(s32[64]{0:T(128)} %param.27) | copy-start | bytes 772
  121.5 8.3 %copy-start.5 = (f32[128,6]{0,1:T(8,128)S(1)}, f32[128,6]{0,1:T(8,128)}, u32[]{:S(2)}) copy-start(f32[128,6]{0,1:T(8,128)} %param.29) | copy-start | bytes 9220
  121.5 157.8 %all-to-all-start.1 = ((bf16[32,2,16,2560]{3,2,1,0:T(8,128)(2,1)}), bf16[32,2,16,2560]{3,2,1,0:T(8,128)(2,1)}, u32[]{:S(2)}, u32[]{:S(2)}) async-start(bf16[32,2,16,2560]{3,2,1,0:T(8,128)(2,1)} %copy.66), calls=%async_computation.1 | async-start | bytes 10485760 | tf_op jit(solution)/shard_map/all_to_all | solution.py:105
  126.6 140.7 %all-reduce.3.cloned.1.call-start = ((), (), s32[]{:S(2)}) async-start(), calls=%async_computation.4 | async-start | bytes 1441792 | tf_op jit(solution)/shard_map/psum | solution.py:56
  129.1 178.2 %reduce-scatter.4.cloned.1.call-start = ((), (), s32[]{:S(2)}) async-start(), calls=%async_computation.3 | async-start | bytes 819200
  129.7 3.8 %copy-start.9 = (bf16[2560,768]{1,0:T(8,128)(2,1)S(1)}, bf16[2560,768]{1,0:T(8,128)(2,1)}, u32[]{:S(2)}) copy-start(bf16[2560,768]{1,0:T(8,128)(2,1)} %param.18) | copy-start | bytes 11796484
  133.5 2.1 copy-start.2
  282.7 3.5 %copy-start.3 = (bf16[16,16,640]{2,0,1:T(8,128)(2,1)S(1)}, bf16[16,16,640]{2,0,1:T(8,128)(2,1)}, u32[]{:S(2)}) copy-start(bf16[16,16,640]{2,0,1:T(8,128)(2,1)} %get-tuple-element.5) | copy-start | bytes 983044
Sparse Core Ops, SparseCore 0:
  130.8 136.4 all-reduce.2
  287.9 19.4 reduce-scatter.3
where the time goes:
time: 316 us
  waiting for transfers between devices  151 us (48%)
  blocking collectives  95.2 us (30%)
  matrix products  31.9 us (10%)
  local copies, waits for them, and re-layouts  14.3 us (5%)
  between operations  13.7 us (4%)
  starting transfers between devices  5.27 us (2%)
  other arithmetic  4.99 us (2%)
    psum x1, waiting for transfers between devices, body(): picked_in, picked_out = lax.psum((picked_in, picked_out), 'dp')  131 us
    all_to_all x1, blocking collectives, body(): lax.all_to_all(send_rows, 'dp', split_axis=0, concat_axis=0, tiled=True)  69.5 us
    unnamed x3, waiting for transfers between devices  19.6 us
    all_gather x1, blocking collectives, body(): gathered = lax.all_gather(hidden, 'mp', axis=1, tiled=True)  14.9 us
    dot_general x1, matrix products, experts_apply(): jnp.einsum('sjcf,jfd->sjcd', inner, expert_down, preferred_element_type=j...  12.8 us
    psum x1, blocking collectives, body(): lowrank_sel = lax.psum(lowrank_sel, 'mp')  10.8 us
    unnamed x25, local copies, waits for them, and re-layouts  7.3 us
  transfers between devices with their start and end apart: 3, of which 2 were waited for; matrix products, arithmetic and copies ran while one was open for 3% of the time, Pallas kernels for 0%

commit v1 on v0

--- a/solution.py
+++ b/solution.py
@@ -2,6 +2,7 @@
 import jax.numpy as jnp
 from jax import lax
 from jax.sharding import PartitionSpec as P
+from jax.lax import all_to_all, axis_size
 
 
 def experts_apply(slots_in, expert_gate, expert_up, expert_down):
@@ -54,7 +55,9 @@
         "ji,ird->jrd", selector, out_cols, preferred_element_type=jnp.float32
     ).astype(jnp.bfloat16)
     picked_in, picked_out = lax.psum((picked_in, picked_out), "dp")
-    gathered = lax.all_gather(hidden, "mp", axis=1, tiled=True)
+    gathered = jnp.concatenate(
+        all_to_all(jnp.stack([hidden for _ in range(axis_size("mp"))]), "mp", 0, 0), axis=1
+    )
     values = gathered.astype(jnp.float32)
     factor = lax.rsqrt(jnp.mean(values * values, axis=-1, keepdims=True) + 1e-06)
     normed = (values * factor * norm_gain.astype(jnp.float32)).astype(jnp.bfloat16)

time: 316 us -> 316 us (level)
  blocking collectives: 95.2 us -> 80.3 us
  waiting for transfers between devices: 151 us -> 157 us
  starting transfers between devices: 5.27 us -> 10.7 us
    all_gather x1 -> x0, blocking collectives: 14.9 us -> none  [body(): gathered = lax.all_gather(hidden, 'mp', axis=1, tiled=True)]
    all_to_all x0 -> x1, waiting for transfers between devices: none -> 5.44 us  [body(): all_to_all(jnp.stack([hidden for _ in range(axis_size('mp'))]), 'mp', 0, 0)]
    all_to_all x0 -> x1, starting transfers between devices: none -> 5.42 us  [body(): all_to_all(jnp.stack([hidden for _ in range(axis_size('mp'))]), 'mp', 0, 0)]
    unnamed x25 -> x24, local copies, waits for them, and re-layouts: 7.3 us -> 7.05 us
  transfers between devices with their start and end apart: 3 -> 4, of which waited for: 2 -> 3; matrix products, arithmetic and copies ran while one was open for 3% -> 5% of each run, Pallas kernels for 0% -> 0%
where the time goes in v1:
time: 316 us
  waiting for transfers between devices  157 us (50%)
  blocking collectives  80.3 us (25%)
  matrix products  33.9 us (11%)
  local copies, waits for them, and re-layouts  14.9 us (5%)
  between operations  13.7 us (4%)
  starting transfers between devices  10.7 us (3%)
  other arithmetic  5.53 us (2%)
    psum x1, waiting for transfers between devices, body(): picked_in, picked_out = lax.psum((picked_in, picked_out), 'dp')  132 us
    all_to_all x1, blocking collectives, body(): lax.all_to_all(send_rows, 'dp', split_axis=0, concat_axis=0, tiled=True)  69.5 us
    unnamed x3, waiting for transfers between devices  19.6 us
    dot_general x1, matrix products, experts_apply(): jnp.einsum('sjcf,jfd->sjcd', inner, expert_down, preferred_element_type=j...  12.8 us
    psum x1, blocking collectives, body(): lowrank_sel = lax.psum(lowrank_sel, 'mp')  10.8 us
    unnamed x24, local copies, waits for them, and re-layouts  7.05 us
  transfers between devices with their start and end apart: 4, of which 3 were waited for; matrix products, arithmetic and copies ran while one was open for 5% of the time, Pallas kernels for 0%

profile of v1, /device:TPU:0, one launch (start us, length us, event | category | flops | bytes accessed | tf_op | source)
XLA Modules:
  0.0 315.8 jit_solution(2823657065508086172)
XLA Ops:
  6.5 0.0 copy-start
  6.5 1.1 copy.63
  7.6 0.9 stack.2
  8.6 5.4 %all-to-all-start = ((bf16[4,128,640]{1,2,0:T(8,128)(2,1)}), bf16[4,128,640]{1,2,0:T(8,128)(2,1)S(1)}, u32[]{:S(2)}, u32[]{:S(2)}) async-start(bf16[4,128,640]{1,2,0:T(8,128)(2,1)} %stack.2), calls=%async_computation | async-start | bytes 1310720 | tf_op jit(solution)/shard_map/all_to_all | solution.py:59
  14.0 0.8 copy.64
  14.8 0.1 eq.85
  14.9 0.1 eq.81
  15.1 1.8 reduce-window.18
  16.9 0.3 slice_reduce_fusion
  17.2 0.1 fusion.34
  17.3 0.1 reduce_sum.58
  17.5 0.1 copy.67
  17.5 0.7 convert_element_type.77
  18.2 0.7 multiply_add_fusion
  18.9 0.5 fusion.9
  19.4 5.4 %all-to-all-done = bf16[4,128,640]{1,2,0:T(8,128)(2,1)S(1)} async-done(((bf16[4,128,640]{1,2,0:T(8,128)(2,1)}), bf16[4,128,640]{1,2,0:T(8,128)(2,1)S(1)}, u32[]{:S(2)}, u32[]{:S(2)}) %all-to-all-start) | async-done | bytes 655392 | tf_op jit(solution)/shard_map/all_to_all | solution.py:59
  24.9 0.4 multiply_reduce_fusion
  25.2 0.4 fusion.23
  25.7 1.6 convolution_convert_fusion
  27.2 0.0 copy-start.8
  27.2 69.5 %all_to_all.15 = bf16[32,2,16,2560]{3,2,1,0:T(8,128)(2,1)S(1)} all-to-all(bf16[32,2,16,2560]{3,2,1,0:T(8,128)(2,1)S(1)} %bitcast.108), channel_id=1, replica_groups=mesh['dp'=32,'mp'=4] {'dp'}, dimensions={0} | all-to-all | bytes 10485760 | tf_op jit(solution)/shard_map/all_to_all | solution.py:110
  96.8 2.3 copy-done.1
  99.1 0.0 copy-done.8
  99.1 2.9 fusion.3
  101.9 12.8 %fusion = bf16[32,2,16,2560]{3,2,0,1:T(8,128)(2,1)} fusion(bf16[2,384,2560]{2,1,0:T(8,128)(2,1)} %param.22, f32[2,32,16,384]{3,2,1,0:T(8,128)S(1)} %fusion.3, bf16[2,2560,384]{2,1,0:T(8,128)(2,1)} %param.21, bf16[32,2,16,2560]{3,2,1,0:T(8,128)(2,1)} %copy-done.1), kind=kOutput, calls=%fused_computation.2 | convolution fusion | flops 4031512576 | bytes 19922944 | tf_op jit(solution)/shard_map/sjcf,jfd->sjcd/dot_general | solution.py:14
  114.7 5.3 %copy.70 = bf16[32,2,16,2560]{3,2,1,0:T(8,128)(2,1)} copy(bf16[32,2,16,2560]{3,2,0,1:T(8,128)(2,1)} %fusion) | data formatting | bytes 10485760 | tf_op jit(solution)/shard_map/convert_element_type | solution.py:114
  120.0 0.0 copy-start.5
  120.0 5.0 %all-to-all-start.2 = ((bf16[32,2,16,2560]{3,2,1,0:T(8,128)(2,1)}), bf16[32,2,16,2560]{3,2,1,0:T(8,128)(2,1)}, u32[]{:S(2)}, u32[]{:S(2)}) async-start(bf16[32,2,16,2560]{3,2,1,0:T(8,128)(2,1)} %copy.70), calls=%async_computation.2 | async-start | bytes 10485760 | tf_op jit(solution)/shard_map/all_to_all | solution.py:108
  125.0 0.0 all-reduce.3.cloned.1.call-start
  125.1 0.0 copy-done.4
  125.1 0.0 copy-done.6
  125.1 0.4 fusion.24
  125.5 0.9 copy.99
  126.4 0.0 copy-done
  126.4 1.1 convolution_convert_fusion.3
  127.5 0.0 all-reduce.3.cloned.1.call-update
  127.6 0.2 reduce-scatter.4.cloned.1.call-start
  127.8 0.0 copy-done.7
  127.8 0.1 copy.71
  127.9 0.1 reduce-window.20
  128.0 0.1 reduce.3
  128.1 0.0 copy-start.2
  128.1 0.1 convert_reduce_fusion
  128.2 0.0 copy-done.9
  128.2 0.1 select_reduce_fusion.1
  128.3 0.0 copy-done.5
  128.3 0.4 select_reduce_fusion
  128.8 3.2 %fusion.55 = f32[128,768]{1,0:T(8,128)S(1)} fusion(bf16[128,2560]{0,1:T(8,128)(2,1)S(1)} %fusion.23, bf16[2560,768]{1,0:T(8,128)(2,1)} %param.17), kind=kOutput, calls=%fused_computation.78 | convolution fusion | flops 503316480 | bytes 4980736 | tf_op jit(solution)/shard_map/dot_general | solution.py:65
  131.9 0.0 copy-done.2
  131.9 0.7 fusion.25
  132.7 131.7 %all-reduce.3.cloned.1.call-done = (bf16[16,16,640]{2,0,1:T(8,128)(2,1)}, bf16[16,16,768]{2,1,0:T(8,128)(2,1)}) async-done(((bf16[16,16,640]{2,0,1:T(8,128)(2,1)}, bf16[16,16,768]{2,1,0:T(8,128)(2,1)}), (bf16[16,16,640]{2,0,1:T(8,128)(2,1)}, bf16[16,16,768]{2,1,0:T(8,128)(2,1)})) %all-reduce.3.cloned.1.call-update) | async-done | bytes 720912 | tf_op jit(solution)/shard_map/psum | solution.py:57
  264.4 1.3 fusion.28
  265.6 10.8 %psum.22 = f32[128,16]{0,1:T(8,128)S(1)} all-reduce(f32[128,16]{0,1:T(8,128)S(1)} %fusion.28), channel_id=1, replica_groups=mesh['dp'=32,'mp'=4] {'mp'}, use_global_device_ids=true, to_apply=%region_11.12 | all-reduce | flops 2048 | bytes 16384 | tf_op jit(solution)/shard_map/psum | solution.py:85
  276.4 2.8 fusion.56
  279.2 0.0 all-to-all-done.2
  279.2 3.3 %fusion.39 = f32[128,2560]{1,0:T(8,128)S(1)} fusion(bf16[1024,2560]{1,0:T(8,128)(2,1)} %bitcast.13, f32[128,1024]{1,0:T(8,128)S(1)} %select_reduce_fusion), kind=kOutput, calls=%fused_computation.53 | convolution fusion | flops 671219712 | bytes 7077888 | tf_op jit(solution)/shard_map/dot_general | solution.py:124
  282.6 0.0 copy-start.3
  282.6 3.5 %fusion.8 = f32[128,2560]{1,0:T(8,128)S(1)} fusion(f32[128,2560]{1,0:T(8,128)S(1)} %fusion.56, f32[128,2560]{1,0:T(8,128)S(1)} %fusion.39, bf16[1024,2560]{1,0:T(8,128)(2,1)} %bitcast.13, f32[128,1024]{1,0:T(8,128)S(1)} %select_reduce_fusion), kind=kOutput, calls=%fused_computation.11 | convolution fusion | flops 672268288 | bytes 9699328 | tf_op jit(solution)/shard_map/dot_general | solution.py:124
  286.1 0.4 fusion.27
  286.5 0.1 convert_element_type.93
  286.5 1.1 copy.79
  287.6 0.0 reduce-scatter.4.cloned.1.call-update
  287.6 19.6 %reduce-scatter.4.cloned.1.call-done = bf16[640,128]{1,0:T(8,128)(2,1)} async-done(((bf16[2560,128]{1,0:T(8,128)(2,1)}), bf16[640,128]{1,0:T(8,128)(2,1)}) %reduce-scatter.4.cloned.1.call-update) | async-done | bytes 163856
  307.2 1.7 copy.80
  (13 shorter events, 0.1 us)
Async XLA Ops:
  6.5 119.9 %copy-start = (bf16[2,16,2560]{2,1,0:T(8,128)(2,1)S(1)}, bf16[2,16,2560]{2,1,0:T(8,128)(2,1)}, u32[]{:S(2)}) copy-start(bf16[2,16,2560]{2,1,0:T(8,128)(2,1)} %param.24) | copy-start | bytes 491524
  8.6 16.3 %all-to-all-start = ((bf16[4,128,640]{1,2,0:T(8,128)(2,1)}), bf16[4,128,640]{1,2,0:T(8,128)(2,1)S(1)}, u32[]{:S(2)}, u32[]{:S(2)}) async-start(bf16[4,128,640]{1,2,0:T(8,128)(2,1)} %stack.2), calls=%async_computation | async-start | bytes 1310720 | tf_op jit(solution)/shard_map/all_to_all | solution.py:59
  27.2 71.9 %copy-start.8 = (bf16[2,2560,384]{2,1,0:T(8,128)(2,1)S(1)}, bf16[2,2560,384]{2,1,0:T(8,128)(2,1)}, u32[]{:S(2)}) copy-start(bf16[2,2560,384]{2,1,0:T(8,128)(2,1)} %param.20) | copy-start | bytes 11796484
  96.8 2.3 copy-start.1
  120.0 5.1 %copy-start.4 = (bf16[2,768,16]{1,2,0:T(8,128)(2,1)S(1)}, bf16[2,768,16]{1,2,0:T(8,128)(2,1)}, u32[]{:S(2)}) copy-start(bf16[2,768,16]{1,2,0:T(8,128)(2,1)} %param.23) | copy-start | bytes 147460
  120.0 5.1 %copy-start.6 = (s32[16]{0:T(128)S(1)}, s32[16]{0:T(128)}, u32[]{:S(2)}) copy-start(s32[16]{0:T(128)} %param.25) | copy-start | bytes 196
  120.0 7.8 %copy-start.7 = (s32[64]{0:T(128)S(1)}, s32[64]{0:T(128)}, u32[]{:S(2)}) copy-start(s32[64]{0:T(128)} %param.26) | copy-start | bytes 772
  120.0 8.3 %copy-start.9 = (s32[64]{0:T(128)S(1)}, s32[64]{0:T(128)}, u32[]{:S(2)}) copy-start(s32[64]{0:T(128)} %param.27) | copy-start | bytes 772
  120.0 8.3 %copy-start.5 = (f32[128,6]{0,1:T(8,128)S(1)}, f32[128,6]{0,1:T(8,128)}, u32[]{:S(2)}) copy-start(f32[128,6]{0,1:T(8,128)} %param.29) | copy-start | bytes 9220
  120.0 159.2 %all-to-all-start.2 = ((bf16[32,2,16,2560]{3,2,1,0:T(8,128)(2,1)}), bf16[32,2,16,2560]{3,2,1,0:T(8,128)(2,1)}, u32[]{:S(2)}, u32[]{:S(2)}) async-start(bf16[32,2,16,2560]{3,2,1,0:T(8,128)(2,1)} %copy.70), calls=%async_computation.2 | async-start | bytes 10485760 | tf_op jit(solution)/shard_map/all_to_all | solution.py:108
  125.0 139.3 %all-reduce.3.cloned.1.call-start = ((), (), s32[]{:S(2)}) async-start(), calls=%async_computation.5 | async-start | bytes 1441792 | tf_op jit(solution)/shard_map/psum | solution.py:57
  127.6 179.7 %reduce-scatter.4.cloned.1.call-start = ((), (), s32[]{:S(2)}) async-start(), calls=%async_computation.4 | async-start | bytes 819200
  128.1 3.8 %copy-start.2 = (bf16[2560,768]{1,0:T(8,128)(2,1)S(1)}, bf16[2560,768]{1,0:T(8,128)(2,1)}, u32[]{:S(2)}) copy-start(bf16[2560,768]{1,0:T(8,128)(2,1)} %param.18) | copy-start | bytes 11796484
  282.6 3.5 %copy-start.3 = (bf16[16,16,640]{2,0,1:T(8,128)(2,1)S(1)}, bf16[16,16,640]{2,0,1:T(8,128)(2,1)}, u32[]{:S(2)}) copy-start(bf16[16,16,640]{2,0,1:T(8,128)(2,1)} %get-tuple-element.5) | copy-start | bytes 983044
Sparse Core Ops, SparseCore 0:
  129.2 135.0 all-reduce.2
  287.8 19.4 reduce-scatter.3
